TPU v7x, 256 devices: a whole 4x4x8 slice. The times are simulated.
256 devices in a mesh: ctx: 32 (over x, y, core), head: 8 (over z).
Axes of the slice: x: 4, y: 4, z: 8, core: 2. Of those that a mesh axis runs over, the one named last changes fastest.
Arguments:
- query_rows: bfloat16 [32, 32768, 128], P('head', 'ctx'), parts along dimension 0, may hold values from -1.75 to 1.75
- key_rows: bfloat16 [32, 32768, 128], P('head', 'ctx'), parts along dimension 0, may hold values from -1.75 to 1.75
- value_rows: bfloat16 [32, 32768, 128], P('head', 'ctx'), parts along dimension 0, may hold values from -6 to 6
- out_grad: bfloat16 [32, 32768, 128], P('head', 'ctx'), parts along dimension 0, may hold values from -6 to 6
- level_gate: float32 [16, 32, 32768], P(None, 'head', 'ctx'), parts along dimension 1, may hold values from -12 to 1
- block_levels: int32 [32, 32], replicated, may hold values from -1 to 15, as said below
Outputs:
- attn_out: bfloat16 [32, 32768, 128], P('head', 'ctx'), parts along dimension 0
- grad_query: bfloat16 [32, 32768, 128], P('head', 'ctx'), parts along dimension 0
- grad_key: bfloat16 [32, 32768, 128], P('head', 'ctx'), parts along dimension 0
- grad_value: bfloat16 [32, 32768, 128], P('head', 'ctx'), parts along dimension 0
- grad_gate: float32 [16, 32, 32768], P(None, 'head', 'ctx'), parts along dimension 1
There are 8 independent parts, one for each index of `head`. A program takes and returns all parts, laid end to end along the dimension named above; an argument that names none is the same for every part. Nothing has to cross between parts.
Inputs may be any that keep to these rules, and one draw needn't show every extreme that they name: The sequence packs documents made of whole blocks; block 0 starts one. block_levels[c, c'] = 10 plus the bit length of (c xor c') where c' < c and both blocks lie in one document, else -1.
All inputs are finite; a program needn't handle non-finite values.
Results may differ from a plain program's by a relative error of at most 0.011.
Values may be sent and summed in bfloat16 or wider, within the bound.
No kernel may reach another device: no remote copies, remote signals or barrier semaphores. Data moves between devices by JAX's collectives and lax.ppermute only.
A program may use at most 128 MiB of HBM per device.

v0:
```python
import jax
import jax.numpy as jnp
from jax import lax
from jax.sharding import PartitionSpec as P


def bit_length(numbers, count):
    total = jnp.zeros(numbers.shape, jnp.int32)
    for shift_by in range(count):
        total = total + (jnp.right_shift(numbers, shift_by) > 0).astype(jnp.int32)
    return total


def head_local(inputs, log_block):
    query_h, key_h, value_h, grad_h, weight_h = inputs
    block_len = query_h.shape[0]
    tile_len = min(64, block_len)
    tile_count = block_len // tile_len
    log_tile = tile_len.bit_length() - 1
    positions = jnp.arange(block_len, dtype=jnp.int32)
    row_tile = positions // tile_len
    row_inner = positions % tile_len
    col_inner = jnp.arange(tile_len, dtype=jnp.int32)
    col_tile = jnp.arange(tile_count, dtype=jnp.int32)
    diag_level = jnp.where(
        col_inner[None, :] <= row_inner[:, None],
        bit_length(jnp.bitwise_xor(row_inner[:, None], col_inner[None, :]), log_tile),
        -1,
    )
    tile_level = jnp.where(
        col_tile[None, :] < row_tile[:, None],
        log_tile
        + bit_length(jnp.bitwise_xor(row_tile[:, None], col_tile[None, :]), log_block - log_tile),
        -1,
    )
    diag_weight = jnp.zeros((block_len, tile_len), jnp.float32)
    for level_num in range(log_tile + 1):
        diag_weight = jnp.where(diag_level == level_num, weight_h[level_num][:, None], diag_weight)
    tile_weight = jnp.zeros((block_len, tile_count), jnp.float32)
    for level_num in range(log_tile + 1, log_block + 1):
        tile_weight = jnp.where(tile_level == level_num, weight_h[level_num][:, None], tile_weight)
    same_tile = row_tile[:, None] == col_tile[None, :]
    mask_weight = jnp.where(
        same_tile[:, :, None], diag_weight[:, None, :], tile_weight[:, :, None]
    ).reshape(block_len, block_len)
    scores = jnp.einsum("td,sd->ts", query_h, key_h, preferred_element_type=jnp.float32)
    probs = (mask_weight * scores).astype(jnp.bfloat16)
    back = jnp.einsum("te,se->ts", grad_h, value_h, preferred_element_type=jnp.float32)
    dprobs = (mask_weight * back).astype(jnp.bfloat16)
    out_inner = jnp.dot(probs, value_h, preferred_element_type=jnp.float32)
    dq_inner = jnp.dot(dprobs, key_h, preferred_element_type=jnp.float32)
    dk_inner = jnp.einsum("ts,td->sd", dprobs, query_h, preferred_element_type=jnp.float32)
    dv_inner = jnp.einsum("ts,te->se", probs, grad_h, preferred_element_type=jnp.float32)
    product = (scores * back).reshape(block_len, tile_count, tile_len)
    tile_sums = jnp.sum(product, axis=2)
    diag_sums = jnp.sum(jnp.where(same_tile[:, :, None], product, jnp.float32(0.0)), axis=1)
    level_terms = []
    for level_num in range(log_block + 1):
        if level_num <= log_tile:
            level_terms.append(
                jnp.sum(jnp.where(diag_level == level_num, diag_sums, jnp.float32(0.0)), axis=1)
            )
        else:
            level_terms.append(
                jnp.sum(jnp.where(tile_level == level_num, tile_sums, jnp.float32(0.0)), axis=1)
            )
    return (out_inner, dq_inner, dk_inner, dv_inner, jnp.stack(level_terms))


def per_device(query_rows, key_rows, value_rows, out_grad, level_gate, block_levels):
    level_total = level_gate.shape[0]
    block_len = query_rows.shape[1]
    log_block = block_len.bit_length() - 1
    log_ctx = level_total - log_block - 1
    stretch_place = lax.axis_index("ctx")
    weights = jnp.exp(level_gate)
    inner_weight = weights[: log_block + 1]
    cross_weight = weights[log_block + 1 :]

    def run_head(inputs):
        return head_local(inputs, log_block)

    local_parts = lax.map(
        run_head, (query_rows, key_rows, value_rows, out_grad, inner_weight.transpose(1, 0, 2))
    )
    out_inner, dq_inner, dk_inner, dv_inner, grad_inner = local_parts
    own_state = jnp.einsum(
        "hcd,hce->hde", key_rows, value_rows, preferred_element_type=jnp.float32
    ).astype(jnp.bfloat16)
    scaled = (cross_weight[..., None] * out_grad[None].astype(jnp.float32)).astype(jnp.bfloat16)
    grad_state = jnp.einsum(
        "hcd,bhce->bhde", query_rows, scaled, preferred_element_type=jnp.float32
    ).astype(jnp.bfloat16)
    levels_row = lax.dynamic_index_in_dim(block_levels, stretch_place, 0, keepdims=False)
    cross_ids = log_block + 1 + jnp.arange(log_ctx, dtype=jnp.int32)
    got = levels_row
    match = got[None, :] == cross_ids[:, None]
    level_sum = jnp.sum(
        jnp.where(
            match[:, :, None, None, None],
            lax.all_gather(own_state[None], "ctx", axis=0, tiled=True)[None].astype(jnp.float32),
            jnp.float32(0.0),
        ),
        axis=1,
    )
    got = levels_row
    match = got[:, None] == cross_ids[None, :]
    key_sum = lax.psum_scatter(
        jnp.sum(
            jnp.where(
                match[:, :, None, None, None],
                grad_state[None].astype(jnp.float32),
                jnp.float32(0.0),
            ),
            axis=1,
        ).astype(jnp.bfloat16),
        "ctx",
        scatter_dimension=0,
        tiled=True,
    ).astype(jnp.float32)[0]
    level_state = level_sum.astype(jnp.bfloat16)
    level_out = jnp.einsum(
        "hcd,bhde->bhce", query_rows, level_state, preferred_element_type=jnp.float32
    )
    level_back = jnp.einsum(
        "hce,bhde->bhcd", out_grad, level_state, preferred_element_type=jnp.float32
    )
    attn = out_inner + jnp.sum(cross_weight[..., None] * level_out, axis=0)
    grad_q = dq_inner + jnp.sum(cross_weight[..., None] * level_back, axis=0)
    grad_cross = cross_weight * jnp.sum(level_out * out_grad[None].astype(jnp.float32), axis=3)
    grad_gate = jnp.concatenate([inner_weight * grad_inner.transpose(1, 0, 2), grad_cross], axis=0)
    key_state = key_sum.astype(jnp.bfloat16)
    grad_k = (
        dk_inner
        + jnp.einsum("hde,hce->hcd", key_state, value_rows, preferred_element_type=jnp.float32)
    ).astype(jnp.bfloat16)
    grad_v = (
        dv_inner
        + jnp.einsum("hde,hcd->hce", key_state, key_rows, preferred_element_type=jnp.float32)
    ).astype(jnp.bfloat16)
    return (attn.astype(jnp.bfloat16), grad_q.astype(jnp.bfloat16), grad_k, grad_v, grad_gate)


def solution(mesh):
    in_specs = (
        P("head", "ctx", None),
        P("head", "ctx", None),
        P("head", "ctx", None),
        P("head", "ctx", None),
        P(None, "head", "ctx"),
        P(),
    )
    out_specs = (
        P("head", "ctx", None),
        P("head", "ctx", None),
        P("head", "ctx", None),
        P("head", "ctx", None),
        P(None, "head", "ctx"),
    )
    return jax.shard_map(
        per_device, mesh=mesh, in_specs=in_specs, out_specs=out_specs, check_vma=False
    )
```

profile of v0, /device:TPU:1, one launch (start us, length us, event | category | flops | bytes accessed | tf_op | source)
XLA Modules:
  0.0 204.0 jit_solution(14055313027224400831)
XLA Ops:
  8.4 1.5 copy.44
  10.0 1.3 copy-done.8
  11.3 3.8 %fusion.47 = f32[5,4,128,128]{2,3,0,1:T(8,128)} fusion(f32[4,1024,128]{1,2,0:T(8,128)S(1)} %copy.44, f32[5,4,1024]{2,0,1:T(8,128)S(1)} %slice.86, bf16[4,1024,128]{2,1,0:T(8,128)(2,1)} %param.8), kind=kOutput, calls=%fused_computation.123 | convolution fusion | flops 676986880 | bytes 4538368 | tf_op jit(solution)/shard_map/hcd,bhce->bhde/dot_general | solution.py:91
  15.1 1.7 copy.45
  16.9 10.4 %select_reduce_fusion.12 = bf16[32,4,128,128]{3,2,1,0:T(8,128)(2,1)} fusion(f32[5,4,128,128]{3,2,1,0:T(8,128)S(1)} %copy.45, pred[32,5]{1,0:T(8,128)(4,1)S(1)} %broadcast_compare_fusion.11), kind=kLoop, calls=%fused_computation.103 | loop fusion | flops 18874368 | bytes 5505184 | tf_op jit(solution)/shard_map/reduce_sum | solution.py:109
  30.1 95.7 %while.20 = (s32[]{:T(128)}, f32[4,1024,128]{1,2,0:T(8,128)}, f32[4,1024,128]{1,2,0:T(8,128)}, f32[4,1024,128]{1,2,0:T(8,128)}, f32[4,1024,128]{1,2,0:T(8,128)},...) while((s32[]{:T(128)}, f32[4,1024,128]{1,2,0:T(8,128)}, ...), condition=%wide.region_14.15_spmd, body=%wide.region_0.14_spmd.sunk | while | flops 1626260480 | bytes 108104296 | solution.py:83
  30.2 1.8 fusion.91
  31.9 5.1 %bitcast_reduce_fusion.2 = (f32[1024,16]{0,1:T(8,128)S(1)}, f32[1024,1024]{0,1:T(8,128)}, f32[1024,1024]{0,1:T(8,128)}) fusion(f32[1024,1024]{0,1:T(8,128)S(1)} %fusion.91, bf16[4,1024,128]{2,1,0:T(8,128)(2,1)S(1)} %get-tuple-element.423, s32[]{:T(128)S(6)} %copy.91, bf16[4,1024,128]{2,1,0:T(8,128)(2,1)} %get-tuple-element.422), kind=kOutput, calls=%fused_computation.clone.1 | convolution fusion | flops 270516224 | bytes 13173760 | tf_op jit(solution)/shard_map/while/body/eval_jaxpr/td,sd->ts/dot_general | solution.py:46
  38.2 3.1 %select_reduce_fusion.18 = (f32[1024,64]{0,1:T(8,128)S(1)}, f32[1024,16,64]{0,2,1:T(8,128)S(1)}) fusion(f32[1024,16,64]{0,2,1:T(8,128)} %bitcast.218, pred[1024,16]{0,1:T(8,128)(4,1)S(1)} %iota_compare_fusion.4, f32[1024,16]{0,1:T(8,128)S(1)} %get-tuple-element.344, f32[1024,64]{0,1:T(8,128)S(1)} %select_select_fusion.3), kind=kLoop, calls=%fused_computation.5.clone.1 | loop fusion | flops 3080192 | bytes 8994816 | tf_op jit(solution)/shard_map/while/body/eval_jaxpr/reduce_sum | solution.py:56
  41.6 1.4 copy-done.4
  43.0 1.8 fusion.93
  44.9 1.3 fusion.94
  46.2 1.3 fusion.95
  47.5 2.6 %fusion.96 = f32[4,1024,128]{1,2,0:T(8,128)} fusion(f32[4,1024,128]{1,2,0:T(8,128)} %get-tuple-element.395, s32[]{:T(128)S(6)} %copy.91, bf16[1024,1024]{0,1:T(8,128)(2,1)S(1)} %get-tuple-element.356, bf16[4,1024,128]{2,1,0:T(8,128)(2,1)} %get-tuple-element.422), kind=kOutput, calls=%fused_computation.10.clone.1 | convolution fusion | flops 268435456 | bytes 2884608 | tf_op jit(solution)/shard_map/while/body/eval_jaxpr/ts,td->sd/dot_general | solution.py:52
  50.2 2.7 %fusion.97 = f32[4,1024,128]{1,2,0:T(8,128)} fusion(f32[4,1024,128]{1,2,0:T(8,128)} %get-tuple-element.396, s32[]{:T(128)S(6)} %copy.91, bf16[1024,1024]{0,1:T(8,128)(2,1)S(1)} %get-tuple-element.355, bf16[4,1024,128]{2,1,0:T(8,128)(2,1)} %get-tuple-element.425), kind=kOutput, calls=%fused_computation.8.clone.1 | convolution fusion | flops 268435456 | bytes 2884608 | tf_op jit(solution)/shard_map/while/body/eval_jaxpr/ts,te->se/dot_general | solution.py:53
  54.1 1.8 fusion.91
  55.8 5.1 %bitcast_reduce_fusion.2 = (f32[1024,16]{0,1:T(8,128)S(1)}, f32[1024,1024]{0,1:T(8,128)}, f32[1024,1024]{0,1:T(8,128)}) fusion(f32[1024,1024]{0,1:T(8,128)S(1)} %fusion.91, bf16[4,1024,128]{2,1,0:T(8,128)(2,1)S(1)} %get-tuple-element.423, s32[]{:T(128)S(6)} %copy.91, bf16[4,1024,128]{2,1,0:T(8,128)(2,1)} %get-tuple-element.422), kind=kOutput, calls=%fused_computation.clone.1 | convolution fusion | flops 270516224 | bytes 13173760 | tf_op jit(solution)/shard_map/while/body/eval_jaxpr/td,sd->ts/dot_general | solution.py:46
  62.1 3.2 %select_reduce_fusion.18 = (f32[1024,64]{0,1:T(8,128)S(1)}, f32[1024,16,64]{0,2,1:T(8,128)S(1)}) fusion(f32[1024,16,64]{0,2,1:T(8,128)} %bitcast.218, pred[1024,16]{0,1:T(8,128)(4,1)S(1)} %iota_compare_fusion.4, f32[1024,16]{0,1:T(8,128)S(1)} %get-tuple-element.344, f32[1024,64]{0,1:T(8,128)S(1)} %select_select_fusion.3), kind=kLoop, calls=%fused_computation.5.clone.1 | loop fusion | flops 3080192 | bytes 8994816 | tf_op jit(solution)/shard_map/while/body/eval_jaxpr/reduce_sum | solution.py:56
  65.8 1.4 copy-done.4
  67.2 1.8 fusion.93
  69.0 1.3 fusion.94
  70.4 1.4 fusion.95
  71.7 2.6 %fusion.96 = f32[4,1024,128]{1,2,0:T(8,128)} fusion(f32[4,1024,128]{1,2,0:T(8,128)} %get-tuple-element.395, s32[]{:T(128)S(6)} %copy.91, bf16[1024,1024]{0,1:T(8,128)(2,1)S(1)} %get-tuple-element.356, bf16[4,1024,128]{2,1,0:T(8,128)(2,1)} %get-tuple-element.422), kind=kOutput, calls=%fused_computation.10.clone.1 | convolution fusion | flops 268435456 | bytes 2884608 | tf_op jit(solution)/shard_map/while/body/eval_jaxpr/ts,td->sd/dot_general | solution.py:52
  74.3 2.7 %fusion.97 = f32[4,1024,128]{1,2,0:T(8,128)} fusion(f32[4,1024,128]{1,2,0:T(8,128)} %get-tuple-element.396, s32[]{:T(128)S(6)} %copy.91, bf16[1024,1024]{0,1:T(8,128)(2,1)S(1)} %get-tuple-element.355, bf16[4,1024,128]{2,1,0:T(8,128)(2,1)} %get-tuple-element.425), kind=kOutput, calls=%fused_computation.8.clone.1 | convolution fusion | flops 268435456 | bytes 2884608 | tf_op jit(solution)/shard_map/while/body/eval_jaxpr/ts,te->se/dot_general | solution.py:53
  78.2 1.7 fusion.91
  80.0 5.1 %bitcast_reduce_fusion.2 = (f32[1024,16]{0,1:T(8,128)S(1)}, f32[1024,1024]{0,1:T(8,128)}, f32[1024,1024]{0,1:T(8,128)}) fusion(f32[1024,1024]{0,1:T(8,128)S(1)} %fusion.91, bf16[4,1024,128]{2,1,0:T(8,128)(2,1)S(1)} %get-tuple-element.423, s32[]{:T(128)S(6)} %copy.91, bf16[4,1024,128]{2,1,0:T(8,128)(2,1)} %get-tuple-element.422), kind=kOutput, calls=%fused_computation.clone.1 | convolution fusion | flops 270516224 | bytes 13173760 | tf_op jit(solution)/shard_map/while/body/eval_jaxpr/td,sd->ts/dot_general | solution.py:46
  86.3 3.2 %select_reduce_fusion.18 = (f32[1024,64]{0,1:T(8,128)S(1)}, f32[1024,16,64]{0,2,1:T(8,128)S(1)}) fusion(f32[1024,16,64]{0,2,1:T(8,128)} %bitcast.218, pred[1024,16]{0,1:T(8,128)(4,1)S(1)} %iota_compare_fusion.4, f32[1024,16]{0,1:T(8,128)S(1)} %get-tuple-element.344, f32[1024,64]{0,1:T(8,128)S(1)} %select_select_fusion.3), kind=kLoop, calls=%fused_computation.5.clone.1 | loop fusion | flops 3080192 | bytes 8994816 | tf_op jit(solution)/shard_map/while/body/eval_jaxpr/reduce_sum | solution.py:56
  89.9 1.4 copy-done.4
  91.2 1.8 fusion.93
  95.7 2.6 %fusion.96 = f32[4,1024,128]{1,2,0:T(8,128)} fusion(f32[4,1024,128]{1,2,0:T(8,128)} %get-tuple-element.395, s32[]{:T(128)S(6)} %copy.91, bf16[1024,1024]{0,1:T(8,128)(2,1)S(1)} %get-tuple-element.356, bf16[4,1024,128]{2,1,0:T(8,128)(2,1)} %get-tuple-element.422), kind=kOutput, calls=%fused_computation.10.clone.1 | convolution fusion | flops 268435456 | bytes 2884608 | tf_op jit(solution)/shard_map/while/body/eval_jaxpr/ts,td->sd/dot_general | solution.py:52
  98.2 2.6 %fusion.97 = f32[4,1024,128]{1,2,0:T(8,128)} fusion(f32[4,1024,128]{1,2,0:T(8,128)} %get-tuple-element.396, s32[]{:T(128)S(6)} %copy.91, bf16[1024,1024]{0,1:T(8,128)(2,1)S(1)} %get-tuple-element.355, bf16[4,1024,128]{2,1,0:T(8,128)(2,1)} %get-tuple-element.425), kind=kOutput, calls=%fused_computation.8.clone.1 | convolution fusion | flops 268435456 | bytes 2884608 | tf_op jit(solution)/shard_map/while/body/eval_jaxpr/ts,te->se/dot_general | solution.py:53
  102.1 1.7 fusion.91
  103.8 5.1 %bitcast_reduce_fusion.2 = (f32[1024,16]{0,1:T(8,128)S(1)}, f32[1024,1024]{0,1:T(8,128)}, f32[1024,1024]{0,1:T(8,128)}) fusion(f32[1024,1024]{0,1:T(8,128)S(1)} %fusion.91, bf16[4,1024,128]{2,1,0:T(8,128)(2,1)S(1)} %get-tuple-element.423, s32[]{:T(128)S(6)} %copy.91, bf16[4,1024,128]{2,1,0:T(8,128)(2,1)} %get-tuple-element.422), kind=kOutput, calls=%fused_computation.clone.1 | convolution fusion | flops 270516224 | bytes 13173760 | tf_op jit(solution)/shard_map/while/body/eval_jaxpr/td,sd->ts/dot_general | solution.py:46
  110.1 3.1 %select_reduce_fusion.18 = (f32[1024,64]{0,1:T(8,128)S(1)}, f32[1024,16,64]{0,2,1:T(8,128)S(1)}) fusion(f32[1024,16,64]{0,2,1:T(8,128)} %bitcast.218, pred[1024,16]{0,1:T(8,128)(4,1)S(1)} %iota_compare_fusion.4, f32[1024,16]{0,1:T(8,128)S(1)} %get-tuple-element.344, f32[1024,64]{0,1:T(8,128)S(1)} %select_select_fusion.3), kind=kLoop, calls=%fused_computation.5.clone.1 | loop fusion | flops 3080192 | bytes 8994816 | tf_op jit(solution)/shard_map/while/body/eval_jaxpr/reduce_sum | solution.py:56
  114.9 1.8 fusion.93
  116.7 1.3 fusion.94
  119.3 2.6 %fusion.96 = f32[4,1024,128]{1,2,0:T(8,128)} fusion(f32[4,1024,128]{1,2,0:T(8,128)} %get-tuple-element.395, s32[]{:T(128)S(6)} %copy.91, bf16[1024,1024]{0,1:T(8,128)(2,1)S(1)} %get-tuple-element.356, bf16[4,1024,128]{2,1,0:T(8,128)(2,1)} %get-tuple-element.422), kind=kOutput, calls=%fused_computation.10.clone.1 | convolution fusion | flops 268435456 | bytes 2884608 | tf_op jit(solution)/shard_map/while/body/eval_jaxpr/ts,td->sd/dot_general | solution.py:52
  121.9 2.6 %fusion.97 = f32[4,1024,128]{1,2,0:T(8,128)} fusion(f32[4,1024,128]{1,2,0:T(8,128)} %get-tuple-element.396, s32[]{:T(128)S(6)} %copy.91, bf16[1024,1024]{0,1:T(8,128)(2,1)S(1)} %get-tuple-element.355, bf16[4,1024,128]{2,1,0:T(8,128)(2,1)} %get-tuple-element.425), kind=kOutput, calls=%fused_computation.8.clone.1 | convolution fusion | flops 268435456 | bytes 2884608 | tf_op jit(solution)/shard_map/while/body/eval_jaxpr/ts,te->se/dot_general | solution.py:53
  126.5 1.7 bitcast_multiply_fusion.5
  128.2 2.1 %fusion.44 = bf16[4,1024,128]{1,2,0:T(8,128)(2,1)S(1)} fusion(f32[4,1024,128]{1,2,0:T(8,128)} %get-tuple-element.151, bf16[4,1024,128]{2,1,0:T(8,128)(2,1)S(1)} %get-tuple-element.440, bf16[1,4,128,128]{3,2,1,0:T(8,128)(2,1)} %reduce-scatter.2.cloned.1.call-done), kind=kOutput, calls=%fused_computation.118 | convolution fusion | flops 135266304 | bytes 4325376 | tf_op jit(solution)/shard_map/hde,hce->hcd/dot_general | solution.py:135
  130.4 1.3 copy.51
  131.7 2.1 %fusion.43 = bf16[4,1024,128]{1,2,0:T(8,128)(2,1)S(1)} fusion(f32[4,1024,128]{1,2,0:T(8,128)} %get-tuple-element.152, bf16[4,1024,128]{2,1,0:T(8,128)(2,1)S(1)} %get-tuple-element.441, bf16[1,4,128,128]{3,2,1,0:T(8,128)(2,1)S(1)} %copy-done.13), kind=kOutput, calls=%fused_computation.116 | convolution fusion | flops 135266304 | bytes 4325376 | tf_op jit(solution)/shard_map/hde,hcd->hce/dot_general | solution.py:139
  135.1 40.2 %all-gather.3.cloned.1.call-done = bf16[128,128,128]{2,1,0:T(8,128)(2,1)} async-done(((bf16[4,128,128]{2,1,0:T(8,128)(2,1)}), bf16[128,128,128]{2,1,0:T(8,128)(2,1)}) %all-gather.3.cloned.1.call-update) | async-done | bytes 4194320 | tf_op jit(solution)/shard_map/all_gather | solution.py:101
  175.3 3.3 %bitcast_convert_fusion = f32[32,4,128,128]{3,2,1,0:T(8,128)S(1)} fusion(bf16[128,128,128]{2,1,0:T(8,128)(2,1)} %all-gather.3.cloned.1.call-done), kind=kLoop, calls=%fused_computation.141 | loop fusion | flops 2097152 | bytes 12582912 | tf_op jit(solution)/shard_map/convert_element_type | solution.py:101
  178.6 5.7 %select_reduce_fusion.13 = bf16[5,4,128,128]{3,2,1,0:T(8,128)(2,1)S(1)} fusion(f32[32,4,128,128]{3,2,1,0:T(8,128)S(1)} %bitcast_convert_fusion, pred[5,32]{1,0:T(8,128)(4,1)S(1)} %broadcast_compare_fusion.12), kind=kLoop, calls=%fused_computation.104 | loop fusion | flops 20643840 | bytes 9044128 | tf_op jit(solution)/shard_map/reduce_sum | solution.py:98
  184.2 3.1 %fusion.37 = f32[4,1024,128]{1,2,0:T(8,128)S(1)} fusion(f32[5,4,1024]{2,0,1:T(8,128)S(1)} %copy-done.18, bf16[4,1024,128]{2,1,0:T(8,128)(2,1)} %param.11, bf16[5,4,128,128]{3,2,1,0:T(8,128)(2,1)S(1)} %select_reduce_fusion.13), kind=kOutput, calls=%fused_computation.106 | convolution fusion | flops 675807232 | bytes 3883008 | tf_op jit(solution)/shard_map/hce,bhde->bhcd/dot_general | solution.py:125
  187.3 3.9 %fusion.39 = (f32[5,4,1024]{2,0,1:T(8,128)S(1)}, f32[4,1024,128]{1,2,0:T(8,128)S(1)}) fusion(f32[4,1024,128]{1,2,0:T(8,128)S(1)} %copy-done.9, f32[5,4,1024]{2,0,1:T(8,128)S(1)} %copy-done.18, bf16[4,1024,128]{2,1,0:T(8,128)(2,1)} %param.8, bf16[5,4,128,128]{3,2,1,0:T(8,128)(2,1)S(1)} %select_reduce_fusion.13), kind=kOutput, calls=%fused_computation.110 | convolution fusion | flops 681029632 | bytes 6062080 | tf_op jit(solution)/shard_map/hcd,bhde->bhce/dot_general | solution.py:122
  191.2 2.4 %add_convert_fusion = (bf16[4,1024,128]{1,2,0:T(8,128)(2,1)S(1)}, bf16[4,1024,128]{1,2,0:T(8,128)(2,1)S(1)}) fusion(f32[4,1024,128]{1,2,0:T(8,128)} %get-tuple-element.150, f32[4,1024,128]{1,2,0:T(8,128)S(1)} %fusion.37, f32[4,1024,128]{1,2,0:T(8,128)S(1)} %copy-done.7, f32[4,1024,128]{1,2,0:T(8,128)S(1)} %get-tuple-element.192), kind=kLoop, calls=%fused_computation.119 | loop fusion | flops 2097152 | bytes 10485760 | tf_op jit(solution)/shard_map/convert_element_type | solution.py:141
  (145 shorter events, 25.6 us)
Async XLA Ops:
  7.2 9.7 %copy-start = (s32[32,32]{1,0:T(8,128)S(1)}, s32[32,32]{1,0:T(8,128)}, u32[]{:S(2)}) copy-start(s32[32,32]{1,0:T(8,128)} %param.13) | copy-start | bytes 12292
  7.2 121.0 %reduce-scatter.2.cloned.1.call-start = ((), (), s32[]{:S(2)}) async-start(), calls=%async_computation.1 | async-start | bytes 4325376 | tf_op jit(solution)/shard_map/reduce_scatter | solution.py:108
  7.2 9.6 %copy-start.19 = (s32[5]{0:T(128)}, s32[5]{0:T(128)S(1)}, u32[]{:S(2)}) copy-start(s32[5]{0:T(128)S(1)} %iota_add_fusion) | copy-start | bytes 64
  8.4 6.7 %copy-start.17 = (f32[5,4,1024]{2,0,1:T(8,128)}, f32[5,4,1024]{2,0,1:T(8,128)S(1)}, u32[]{:S(2)}) copy-start(f32[5,4,1024]{2,0,1:T(8,128)S(1)} %slice.86) | copy-start | bytes 245764
  10.0 1.3 copy-start.8
  16.9 10.5 %copy-start.20 = (s32[32]{0:T(128)}, s32[32]{0:T(128)S(1)}, u32[]{:S(2)}) copy-start(s32[32]{0:T(128)S(1)} %dynamic-slice_bitcast_fusion) | copy-start | bytes 388
  27.4 1.2 copy-start.5
  27.4 1.5 copy-start.6
  27.4 147.9 %all-gather.3.cloned.1.call-start = ((), (), s32[]{:S(2)}) async-start(), calls=%async_computation.2 | async-start | bytes 4325376 | tf_op jit(solution)/shard_map/all_gather | solution.py:101
  30.1 6.9 %copy-start.11 = (f32[4,11,1024]{2,1,0:T(8,128)}, f32[4,11,1024]{2,1,0:T(8,128)S(1)}, u32[]{:S(2)}) copy-start(f32[4,11,1024]{2,1,0:T(8,128)S(1)} %get-tuple-element.421) | copy-start | bytes 540676 | tf_op jit(solution)/shard_map/while
  31.9 5.1 %copy-start.2 = (f32[1024,1024]{0,1:T(8,128)}, f32[1024,1024]{0,1:T(8,128)S(1)}, u32[]{:S(2)}) copy-start(f32[1024,1024]{0,1:T(8,128)S(1)} %fusion.91) | copy-start | bytes 12582916 | tf_op jit(solution)/shard_map/while
  38.2 3.5 %copy-start.3 = (f32[1024,1024]{0,1:T(8,128)S(1)}, f32[1024,1024]{0,1:T(8,128)}, u32[]{:S(2)}) copy-start(f32[1024,1024]{0,1:T(8,128)} %copy-done.2) | copy-start | bytes 12582916 | tf_op jit(solution)/shard_map/while
  38.2 4.8 %copy-start.4 = (f32[1024,1024]{0,1:T(8,128)S(1)}, f32[1024,1024]{0,1:T(8,128)}, u32[]{:S(2)}) copy-start(f32[1024,1024]{0,1:T(8,128)} %get-tuple-element.354) | copy-start | bytes 12582916 | tf_op jit(solution)/shard_map/while
  50.1 3.1 %copy-start.14 = (f32[1024]{0:T(1024)S(1)}, f32[1024]{0:T(1024)}, u32[]{:S(2)}) copy-start(f32[1024]{0:T(1024)} %get-tuple-element.367) | copy-start | bytes 12292 | tf_op jit(solution)/shard_map/while
  50.2 3.1 %copy-start.15 = (f32[1024]{0:T(1024)S(1)}, f32[1024]{0:T(1024)}, u32[]{:S(2)}) copy-start(f32[1024]{0:T(1024)} %get-tuple-element.366) | copy-start | bytes 12292 | tf_op jit(solution)/shard_map/while
  50.2 3.2 %copy-start.16 = (f32[1024]{0:T(1024)S(1)}, f32[1024]{0:T(1024)}, u32[]{:S(2)}) copy-start(f32[1024]{0:T(1024)} %get-tuple-element.365) | copy-start | bytes 12292 | tf_op jit(solution)/shard_map/while
  50.2 3.9 %copy-start.12 = (f32[4,11,1024]{2,1,0:T(8,128)S(1)}, f32[4,11,1024]{2,1,0:T(8,128)}, u32[]{:S(2)}) copy-start(f32[4,11,1024]{2,1,0:T(8,128)} %copy-done.11) | copy-start | bytes 540676 | tf_op jit(solution)/shard_map/while
  54.1 6.9 %copy-start.11 = (f32[4,11,1024]{2,1,0:T(8,128)}, f32[4,11,1024]{2,1,0:T(8,128)S(1)}, u32[]{:S(2)}) copy-start(f32[4,11,1024]{2,1,0:T(8,128)S(1)} %get-tuple-element.421) | copy-start | bytes 540676 | tf_op jit(solution)/shard_map/while
  55.8 5.1 %copy-start.2 = (f32[1024,1024]{0,1:T(8,128)}, f32[1024,1024]{0,1:T(8,128)S(1)}, u32[]{:S(2)}) copy-start(f32[1024,1024]{0,1:T(8,128)S(1)} %fusion.91) | copy-start | bytes 12582916 | tf_op jit(solution)/shard_map/while
  62.1 3.7 %copy-start.3 = (f32[1024,1024]{0,1:T(8,128)S(1)}, f32[1024,1024]{0,1:T(8,128)}, u32[]{:S(2)}) copy-start(f32[1024,1024]{0,1:T(8,128)} %copy-done.2) | copy-start | bytes 12582916 | tf_op jit(solution)/shard_map/while
  62.1 5.1 %copy-start.4 = (f32[1024,1024]{0,1:T(8,128)S(1)}, f32[1024,1024]{0,1:T(8,128)}, u32[]{:S(2)}) copy-start(f32[1024,1024]{0,1:T(8,128)} %get-tuple-element.354) | copy-start | bytes 12582916 | tf_op jit(solution)/shard_map/while
  74.3 3.1 %copy-start.14 = (f32[1024]{0:T(1024)S(1)}, f32[1024]{0:T(1024)}, u32[]{:S(2)}) copy-start(f32[1024]{0:T(1024)} %get-tuple-element.367) | copy-start | bytes 12292 | tf_op jit(solution)/shard_map/while
  74.3 3.2 %copy-start.15 = (f32[1024]{0:T(1024)S(1)}, f32[1024]{0:T(1024)}, u32[]{:S(2)}) copy-start(f32[1024]{0:T(1024)} %get-tuple-element.366) | copy-start | bytes 12292 | tf_op jit(solution)/shard_map/while
  74.3 3.2 %copy-start.16 = (f32[1024]{0:T(1024)S(1)}, f32[1024]{0:T(1024)}, u32[]{:S(2)}) copy-start(f32[1024]{0:T(1024)} %get-tuple-element.365) | copy-start | bytes 12292 | tf_op jit(solution)/shard_map/while
  74.3 3.9 %copy-start.12 = (f32[4,11,1024]{2,1,0:T(8,128)S(1)}, f32[4,11,1024]{2,1,0:T(8,128)}, u32[]{:S(2)}) copy-start(f32[4,11,1024]{2,1,0:T(8,128)} %copy-done.11) | copy-start | bytes 540676 | tf_op jit(solution)/shard_map/while
  78.2 6.9 %copy-start.11 = (f32[4,11,1024]{2,1,0:T(8,128)}, f32[4,11,1024]{2,1,0:T(8,128)S(1)}, u32[]{:S(2)}) copy-start(f32[4,11,1024]{2,1,0:T(8,128)S(1)} %get-tuple-element.421) | copy-start | bytes 540676 | tf_op jit(solution)/shard_map/while
  80.0 5.1 %copy-start.2 = (f32[1024,1024]{0,1:T(8,128)}, f32[1024,1024]{0,1:T(8,128)S(1)}, u32[]{:S(2)}) copy-start(f32[1024,1024]{0,1:T(8,128)S(1)} %fusion.91) | copy-start | bytes 12582916 | tf_op jit(solution)/shard_map/while
  86.3 3.6 %copy-start.3 = (f32[1024,1024]{0,1:T(8,128)S(1)}, f32[1024,1024]{0,1:T(8,128)}, u32[]{:S(2)}) copy-start(f32[1024,1024]{0,1:T(8,128)} %copy-done.2) | copy-start | bytes 12582916 | tf_op jit(solution)/shard_map/while
  86.3 4.9 %copy-start.4 = (f32[1024,1024]{0,1:T(8,128)S(1)}, f32[1024,1024]{0,1:T(8,128)}, u32[]{:S(2)}) copy-start(f32[1024,1024]{0,1:T(8,128)} %get-tuple-element.354) | copy-start | bytes 12582916 | tf_op jit(solution)/shard_map/while
  98.2 3.1 %copy-start.14 = (f32[1024]{0:T(1024)S(1)}, f32[1024]{0:T(1024)}, u32[]{:S(2)}) copy-start(f32[1024]{0:T(1024)} %get-tuple-element.367) | copy-start | bytes 12292 | tf_op jit(solution)/shard_map/while
  98.2 3.1 %copy-start.15 = (f32[1024]{0:T(1024)S(1)}, f32[1024]{0:T(1024)}, u32[]{:S(2)}) copy-start(f32[1024]{0:T(1024)} %get-tuple-element.366) | copy-start | bytes 12292 | tf_op jit(solution)/shard_map/while
  98.2 3.1 %copy-start.16 = (f32[1024]{0:T(1024)S(1)}, f32[1024]{0:T(1024)}, u32[]{:S(2)}) copy-start(f32[1024]{0:T(1024)} %get-tuple-element.365) | copy-start | bytes 12292 | tf_op jit(solution)/shard_map/while
  98.2 3.8 %copy-start.12 = (f32[4,11,1024]{2,1,0:T(8,128)S(1)}, f32[4,11,1024]{2,1,0:T(8,128)}, u32[]{:S(2)}) copy-start(f32[4,11,1024]{2,1,0:T(8,128)} %copy-done.11) | copy-start | bytes 540676 | tf_op jit(solution)/shard_map/while
  102.1 6.9 %copy-start.11 = (f32[4,11,1024]{2,1,0:T(8,128)}, f32[4,11,1024]{2,1,0:T(8,128)S(1)}, u32[]{:S(2)}) copy-start(f32[4,11,1024]{2,1,0:T(8,128)S(1)} %get-tuple-element.421) | copy-start | bytes 540676 | tf_op jit(solution)/shard_map/while
  103.8 5.1 %copy-start.2 = (f32[1024,1024]{0,1:T(8,128)}, f32[1024,1024]{0,1:T(8,128)S(1)}, u32[]{:S(2)}) copy-start(f32[1024,1024]{0,1:T(8,128)S(1)} %fusion.91) | copy-start | bytes 12582916 | tf_op jit(solution)/shard_map/while
  110.1 3.5 %copy-start.3 = (f32[1024,1024]{0,1:T(8,128)S(1)}, f32[1024,1024]{0,1:T(8,128)}, u32[]{:S(2)}) copy-start(f32[1024,1024]{0,1:T(8,128)} %copy-done.2) | copy-start | bytes 12582916 | tf_op jit(solution)/shard_map/while
  110.1 4.8 %copy-start.4 = (f32[1024,1024]{0,1:T(8,128)S(1)}, f32[1024,1024]{0,1:T(8,128)}, u32[]{:S(2)}) copy-start(f32[1024,1024]{0,1:T(8,128)} %get-tuple-element.354) | copy-start | bytes 12582916 | tf_op jit(solution)/shard_map/while
  121.9 3.1 %copy-start.14 = (f32[1024]{0:T(1024)S(1)}, f32[1024]{0:T(1024)}, u32[]{:S(2)}) copy-start(f32[1024]{0:T(1024)} %get-tuple-element.367) | copy-start | bytes 12292 | tf_op jit(solution)/shard_map/while
  121.9 3.1 %copy-start.15 = (f32[1024]{0:T(1024)S(1)}, f32[1024]{0:T(1024)}, u32[]{:S(2)}) copy-start(f32[1024]{0:T(1024)} %get-tuple-element.366) | copy-start | bytes 12292 | tf_op jit(solution)/shard_map/while
  121.9 3.1 %copy-start.16 = (f32[1024]{0:T(1024)S(1)}, f32[1024]{0:T(1024)}, u32[]{:S(2)}) copy-start(f32[1024]{0:T(1024)} %get-tuple-element.365) | copy-start | bytes 12292 | tf_op jit(solution)/shard_map/while
  121.9 3.9 %copy-start.12 = (f32[4,11,1024]{2,1,0:T(8,128)S(1)}, f32[4,11,1024]{2,1,0:T(8,128)}, u32[]{:S(2)}) copy-start(f32[4,11,1024]{2,1,0:T(8,128)} %copy-done.11) | copy-start | bytes 540676 | tf_op jit(solution)/shard_map/while
  130.3 1.3 copy-start.13
  178.5 5.7 %copy-start.18 = (f32[5,4,1024]{2,0,1:T(8,128)S(1)}, f32[5,4,1024]{2,0,1:T(8,128)}, u32[]{:S(2)}) copy-start(f32[5,4,1024]{2,0,1:T(8,128)} %copy-done.17) | copy-start | bytes 245764
  184.2 3.1 %copy-start.9 = (f32[4,1024,128]{1,2,0:T(8,128)S(1)}, f32[4,1024,128]{1,2,0:T(8,128)}, u32[]{:S(2)}) copy-start(f32[4,1024,128]{1,2,0:T(8,128)} %copy-done.8) | copy-start | bytes 6291460
  187.3 3.9 %copy-start.7 = (f32[4,1024,128]{1,2,0:T(8,128)S(1)}, f32[4,1024,128]{1,2,0:T(8,128)}, u32[]{:S(2)}) copy-start(f32[4,1024,128]{1,2,0:T(8,128)} %get-tuple-element.149) | copy-start | bytes 6291460
  193.6 2.7 %copy-start.10 = (f32[11,4,1024]{2,0,1:T(8,128)S(1)}, f32[11,4,1024]{2,0,1:T(8,128)}, u32[]{:S(2)}) copy-start(f32[11,4,1024]{2,0,1:T(8,128)} %bitcast_multiply_fusion.5) | copy-start | bytes 540676
  193.6 3.6 %copy-start.1 = (s32[32,32]{1,0:T(8,128)S(1)}, s32[32,32]{1,0:T(8,128)}, u32[]{:S(2)}) copy-start(s32[32,32]{1,0:T(8,128)} %param.13) | copy-start | bytes 12292
Sparse Core Ops, SparseCore 0:
  27.5 91.6 reduce-scatter.1
  122.7 52.5 all-gather.2
where the time goes:
time: 205 us; the launch traced here: 204 us
  matrix products  75.1 us (37%)
  other arithmetic  50.3 us (25%)
  waiting for transfers between devices  40.3 us (20%)
  local copies, waits for them, and re-layouts  23.4 us (11%)
  between operations  14.3 us (7%)
    all_gather x1, waiting for transfers between devices, per_device(): lax.all_gather(own_state[None], 'ctx', axis=0, tiled=True)[None]  40.2 us
    dot_general x4, matrix products, head_local(): jnp.einsum('td,sd->ts', query_h, key_h, preferred_element_type=jnp.float32)  20.5 us
    reduce_sum x4, other arithmetic, head_local(): jnp.sum(jnp.where(same_tile[:, :, None], product, jnp.float32(0.0)), axis=1)  12.6 us
    dot_general x4, matrix products, head_local(): jnp.einsum('ts,te->se', probs, grad_h, preferred_element_type=jnp.float32)  10.6 us
    reduce_sum x1, other arithmetic, per_device(): jnp.sum(jnp.where(match[:, :, None, None, None], grad_state[None].astype(...  10.4 us
    dot_general x4, matrix products, head_local(): jnp.einsum('ts,td->sd', dprobs, query_h, preferred_element_type=jnp.float32)  10.4 us
    unnamed x31, local copies, waits for them, and re-layouts  8.76 us
    convert_element_type x4, other arithmetic, head_local(): dprobs = (mask_weight * back).astype(jnp.bfloat16)  7.39 us
  transfers between devices with their start and end apart: 2, of which 1 were waited for; matrix products, arithmetic and copies ran while one was open for 48% of the time, Pallas kernels for 0%

commit v1 on v0

--- a/solution.py
+++ b/solution.py
@@ -98,7 +98,10 @@
     level_sum = jnp.sum(
         jnp.where(
             match[:, :, None, None, None],
-            lax.all_gather(own_state[None], "ctx", axis=0, tiled=True)[None].astype(jnp.float32),
+            jnp.concatenate(
+                lax.all_to_all(jnp.stack([own_state[None]] * lax.axis_size("ctx")), "ctx", 0, 0),
+                axis=0,
+            )[None].astype(jnp.float32),
             jnp.float32(0.0),
         ),
         axis=1,

time: 205 us -> 173 us (0.84)
  waiting for transfers between devices: 40.3 us -> 0.02 us
  starting transfers between devices: 0.26 us -> 8.81 us
  matrix products: 75.1 us -> 66.8 us
  local copies, waits for them, and re-layouts: 23.4 us -> 30 us
    all_gather x1 -> x0, waiting for transfers between devices: 40.2 us -> none  [per_device(): lax.all_gather(own_state[None], 'ctx', axis=0, tiled=True)[None]]
    all_to_all x0 -> x1, starting transfers between devices: none -> 8.77 us  [per_device(): lax.all_to_all(jnp.stack([own_state[None]] * lax.axis_size('ctx')), 'ctx'...]
    slice x4, local copies, waits for them, and re-layouts: 0.24 us -> 4.49 us  [head_local(): weight_h[level_num][:, None]]
    dot_general x4, matrix products: 7 us -> 2.81 us  [head_local(): jnp.einsum('te,se->ts', grad_h, value_h, preferred_element_type=jnp.float32)]
    dot_general x4, matrix products: 10.6 us -> 6.56 us  [head_local(): jnp.einsum('ts,te->se', probs, grad_h, preferred_element_type=jnp.float32)]
    another operation x0 -> x1, local copies, waits for them, and re-layouts: none -> 3.02 us  [per_device(): jnp.stack([own_state[None]] * lax.axis_size('ctx'))]
    unnamed x31 -> x37, local copies, waits for them, and re-layouts: 8.76 us -> 8.3 us
    while x64 -> x56, local copies, waits for them, and re-layouts: 7.02 us -> 6.91 us
  transfers between devices with their start and end apart: 2 -> 2, of which waited for: 1 -> 0; matrix products, arithmetic and copies ran while one was open for 48% -> 75% of each run, Pallas kernels for 0% -> 0%
where the time goes in v1:
time: 173 us; the launch traced here: 172 us
  matrix products  66.8 us (39%)
  other arithmetic  51.4 us (30%)
  local copies, waits for them, and re-layouts  30 us (17%)
  between operations  14.3 us (8%)
  starting transfers between devices  8.81 us (5%)
    dot_general x4, matrix products, head_local(): jnp.einsum('td,sd->ts', query_h, key_h, preferred_element_type=jnp.float32)  20.6 us
    reduce_sum x4, other arithmetic, head_local(): jnp.sum(jnp.where(same_tile[:, :, None], product, jnp.float32(0.0)), axis=1)  12.6 us
    dot_general x4, matrix products, head_local(): jnp.einsum('ts,td->sd', dprobs, query_h, preferred_element_type=jnp.float32)  10.7 us
    reduce_sum x1, other arithmetic, per_device(): jnp.sum(jnp.where(match[:, :, None, None, None], grad_state[None].astype(...  10.4 us
    all_to_all x1, starting transfers between devices, per_device(): lax.all_to_all(jnp.stack([own_state[None]] * lax.axis_size('ctx')), 'ctx'...  8.77 us
    unnamed x37, local copies, waits for them, and re-layouts  8.3 us
    convert_element_type x4, other arithmetic, head_local(): dprobs = (mask_weight * back).astype(jnp.bfloat16)  7.39 us
    while x56, local copies, waits for them, and re-layouts  6.91 us
  transfers between devices with their start and end apart: 2, of which 0 were waited for; matrix products, arithmetic and copies ran while one was open for 75% of the time, Pallas kernels for 0%

profile of v1, /device:TPU:1, one launch (start us, length us, event | category | flops | bytes accessed | tf_op | source)
XLA Modules:
  0.0 171.7 jit_solution(628673971338421054)
XLA Ops:
  7.2 2.0 %convolution_convert_fusion = bf16[4,128,128]{2,1,0:T(8,128)(2,1)S(1)} fusion(bf16[4,1024,128]{2,1,0:T(8,128)(2,1)} %param.9, bf16[4,1024,128]{2,1,0:T(8,128)(2,1)} %param.10), kind=kOutput, calls=%fused_computation.125 | convolution fusion | flops 134283264 | bytes 2228224 | tf_op jit(solution)/shard_map/hcd,hce->hde/dot_general | solution.py:87
  9.2 3.0 %stack.75 = bf16[32,1,4,128,128]{4,3,2,1,0:T(8,128)(2,1)} broadcast(bf16[4,128,128]{2,1,0:T(8,128)(2,1)S(1)} %convolution_convert_fusion), dimensions={2,3,4} | broadcast | bytes 4325376 | tf_op jit(solution)/shard_map/stack | solution.py:102
  12.2 8.8 %all-to-all-start = ((bf16[32,1,4,128,128]{4,3,2,1,0:T(8,128)(2,1)}), bf16[32,1,4,128,128]{4,3,2,1,0:T(8,128)(2,1)}, u32[]{:S(2)}, u32[]{:S(2)}) async-start(bf16[32,1,4,128,128]{4,3,2,1,0:T(8,128)(2,1)} %stack.75), calls=%async_computation | async-start | bytes 8388608 | tf_op jit(solution)/shard_map/all_to_all | solution.py:102
  21.3 1.7 copy.44
  23.0 4.3 %fusion.47 = f32[5,4,128,128]{2,3,0,1:T(8,128)} fusion(f32[4,1024,128]{1,2,0:T(8,128)} %copy.44, f32[5,4,1024]{2,0,1:T(8,128)S(1)} %slice.86, bf16[4,1024,128]{2,1,0:T(8,128)(2,1)S(1)} %copy-done.9), kind=kOutput, calls=%fused_computation.124 | convolution fusion | flops 676986880 | bytes 4538368 | tf_op jit(solution)/shard_map/hcd,bhce->bhde/dot_general | solution.py:91
  27.3 1.7 copy.45
  29.2 10.4 %select_reduce_fusion.12 = bf16[32,4,128,128]{3,2,1,0:T(8,128)(2,1)} fusion(f32[5,4,128,128]{3,2,1,0:T(8,128)S(1)} %copy.45, pred[32,5]{1,0:T(8,128)(4,1)S(1)} %broadcast_compare_fusion.11), kind=kLoop, calls=%fused_computation.103 | loop fusion | flops 18874368 | bytes 5505184 | tf_op jit(solution)/shard_map/reduce_sum | solution.py:112
  41.2 92.0 %while.20 = (s32[]{:T(128)}, f32[4,1024,128]{1,2,0:T(8,128)}, f32[4,1024,128]{1,2,0:T(8,128)}, f32[4,1024,128]{1,2,0:T(8,128)}, f32[4,1024,128]{1,2,0:T(8,128)},...) while((s32[]{:T(128)}, f32[4,1024,128]{1,2,0:T(8,128)}, ...), condition=%wide.region_14.15_spmd, body=%wide.region_0.14_spmd.sunk | while | flops 1626260480 | bytes 110856792 | solution.py:83
  41.9 5.1 %bitcast_reduce_fusion.2 = (f32[1024,16]{0,1:T(8,128)S(1)}, f32[1024,1024]{0,1:T(8,128)}, f32[1024,1024]{0,1:T(8,128)}) fusion(f32[1024,1024]{0,1:T(8,128)S(1)} %fusion.91, bf16[4,1024,128]{2,1,0:T(8,128)(2,1)S(1)} %get-tuple-element.423, s32[]{:T(128)S(6)} %copy.91, bf16[4,1024,128]{2,1,0:T(8,128)(2,1)} %get-tuple-element.422), kind=kOutput, calls=%fused_computation.clone.1 | convolution fusion | flops 270516224 | bytes 13173760 | tf_op jit(solution)/shard_map/while/body/eval_jaxpr/td,sd->ts/dot_general | solution.py:46
  49.3 3.1 %select_reduce_fusion.18 = (f32[1024,64]{0,1:T(8,128)S(1)}, f32[1024,16,64]{0,2,1:T(8,128)S(1)}) fusion(f32[1024,16,64]{0,2,1:T(8,128)} %bitcast.218, pred[1024,16]{0,1:T(8,128)(4,1)S(1)} %iota_compare_fusion.4, f32[1024,16]{0,1:T(8,128)S(1)} %get-tuple-element.344, f32[1024,64]{0,1:T(8,128)S(1)} %select_select_fusion.3), kind=kLoop, calls=%fused_computation.5.clone.1 | loop fusion | flops 3080192 | bytes 8994816 | tf_op jit(solution)/shard_map/while/body/eval_jaxpr/reduce_sum | solution.py:56
  52.7 1.4 copy-done.4
  54.1 1.8 %fusion.93 = (bf16[1024,1024]{0,1:T(8,128)(2,1)S(1)}, bf16[1024,1024]{0,1:T(8,128)(2,1)S(1)}) fusion(f32[1024,1024]{0,1:T(8,128)S(1)} %copy-done.3, f32[1024,16,64]{0,2,1:T(8,128)S(1)} %get-tuple-element.353, f32[1024,1024]{0,1:T(8,128)S(1)} %copy-done.4), kind=kLoop, calls=%fused_computation.4.clone.1 | loop fusion | flops 4194304 | bytes 16777216 | tf_op jit(solution)/shard_map/while/body/eval_jaxpr/convert_element_type | solution.py:49
  55.9 1.3 fusion.94
  57.3 1.3 fusion.95
  58.6 2.7 %fusion.96 = f32[4,1024,128]{1,2,0:T(8,128)} fusion(f32[4,1024,128]{1,2,0:T(8,128)} %get-tuple-element.395, s32[]{:T(128)S(6)} %copy.91, bf16[1024,1024]{0,1:T(8,128)(2,1)S(1)} %get-tuple-element.356, bf16[4,1024,128]{2,1,0:T(8,128)(2,1)} %get-tuple-element.422), kind=kOutput, calls=%fused_computation.10.clone.1 | convolution fusion | flops 268435456 | bytes 2884608 | tf_op jit(solution)/shard_map/while/body/eval_jaxpr/ts,td->sd/dot_general | solution.py:52
  61.3 1.6 fusion.97
  64.9 5.2 %bitcast_reduce_fusion.2 = (f32[1024,16]{0,1:T(8,128)S(1)}, f32[1024,1024]{0,1:T(8,128)}, f32[1024,1024]{0,1:T(8,128)}) fusion(f32[1024,1024]{0,1:T(8,128)S(1)} %fusion.91, bf16[4,1024,128]{2,1,0:T(8,128)(2,1)S(1)} %get-tuple-element.423, s32[]{:T(128)S(6)} %copy.91, bf16[4,1024,128]{2,1,0:T(8,128)(2,1)} %get-tuple-element.422), kind=kOutput, calls=%fused_computation.clone.1 | convolution fusion | flops 270516224 | bytes 13173760 | tf_op jit(solution)/shard_map/while/body/eval_jaxpr/td,sd->ts/dot_general | solution.py:46
  72.3 3.2 %select_reduce_fusion.18 = (f32[1024,64]{0,1:T(8,128)S(1)}, f32[1024,16,64]{0,2,1:T(8,128)S(1)}) fusion(f32[1024,16,64]{0,2,1:T(8,128)} %bitcast.218, pred[1024,16]{0,1:T(8,128)(4,1)S(1)} %iota_compare_fusion.4, f32[1024,16]{0,1:T(8,128)S(1)} %get-tuple-element.344, f32[1024,64]{0,1:T(8,128)S(1)} %select_select_fusion.3), kind=kLoop, calls=%fused_computation.5.clone.1 | loop fusion | flops 3080192 | bytes 8994816 | tf_op jit(solution)/shard_map/while/body/eval_jaxpr/reduce_sum | solution.py:56
  75.9 1.4 copy-done.4
  77.3 1.8 %fusion.93 = (bf16[1024,1024]{0,1:T(8,128)(2,1)S(1)}, bf16[1024,1024]{0,1:T(8,128)(2,1)S(1)}) fusion(f32[1024,1024]{0,1:T(8,128)S(1)} %copy-done.3, f32[1024,16,64]{0,2,1:T(8,128)S(1)} %get-tuple-element.353, f32[1024,1024]{0,1:T(8,128)S(1)} %copy-done.4), kind=kLoop, calls=%fused_computation.4.clone.1 | loop fusion | flops 4194304 | bytes 16777216 | tf_op jit(solution)/shard_map/while/body/eval_jaxpr/convert_element_type | solution.py:49
  79.2 1.3 fusion.94
  80.5 1.4 fusion.95
  81.9 2.7 %fusion.96 = f32[4,1024,128]{1,2,0:T(8,128)} fusion(f32[4,1024,128]{1,2,0:T(8,128)} %get-tuple-element.395, s32[]{:T(128)S(6)} %copy.91, bf16[1024,1024]{0,1:T(8,128)(2,1)S(1)} %get-tuple-element.356, bf16[4,1024,128]{2,1,0:T(8,128)(2,1)} %get-tuple-element.422), kind=kOutput, calls=%fused_computation.10.clone.1 | convolution fusion | flops 268435456 | bytes 2884608 | tf_op jit(solution)/shard_map/while/body/eval_jaxpr/ts,td->sd/dot_general | solution.py:52
  84.5 1.6 fusion.97
  88.1 5.2 %bitcast_reduce_fusion.2 = (f32[1024,16]{0,1:T(8,128)S(1)}, f32[1024,1024]{0,1:T(8,128)}, f32[1024,1024]{0,1:T(8,128)}) fusion(f32[1024,1024]{0,1:T(8,128)S(1)} %fusion.91, bf16[4,1024,128]{2,1,0:T(8,128)(2,1)S(1)} %get-tuple-element.423, s32[]{:T(128)S(6)} %copy.91, bf16[4,1024,128]{2,1,0:T(8,128)(2,1)} %get-tuple-element.422), kind=kOutput, calls=%fused_computation.clone.1 | convolution fusion | flops 270516224 | bytes 13173760 | tf_op jit(solution)/shard_map/while/body/eval_jaxpr/td,sd->ts/dot_general | solution.py:46
  95.5 3.1 %select_reduce_fusion.18 = (f32[1024,64]{0,1:T(8,128)S(1)}, f32[1024,16,64]{0,2,1:T(8,128)S(1)}) fusion(f32[1024,16,64]{0,2,1:T(8,128)} %bitcast.218, pred[1024,16]{0,1:T(8,128)(4,1)S(1)} %iota_compare_fusion.4, f32[1024,16]{0,1:T(8,128)S(1)} %get-tuple-element.344, f32[1024,64]{0,1:T(8,128)S(1)} %select_select_fusion.3), kind=kLoop, calls=%fused_computation.5.clone.1 | loop fusion | flops 3080192 | bytes 8994816 | tf_op jit(solution)/shard_map/while/body/eval_jaxpr/reduce_sum | solution.py:56
  99.0 1.3 copy-done.4
  100.3 1.8 %fusion.93 = (bf16[1024,1024]{0,1:T(8,128)(2,1)S(1)}, bf16[1024,1024]{0,1:T(8,128)(2,1)S(1)}) fusion(f32[1024,1024]{0,1:T(8,128)S(1)} %copy-done.3, f32[1024,16,64]{0,2,1:T(8,128)S(1)} %get-tuple-element.353, f32[1024,1024]{0,1:T(8,128)S(1)} %copy-done.4), kind=kLoop, calls=%fused_computation.4.clone.1 | loop fusion | flops 4194304 | bytes 16777216 | tf_op jit(solution)/shard_map/while/body/eval_jaxpr/convert_element_type | solution.py:49
  104.7 2.7 %fusion.96 = f32[4,1024,128]{1,2,0:T(8,128)} fusion(f32[4,1024,128]{1,2,0:T(8,128)} %get-tuple-element.395, s32[]{:T(128)S(6)} %copy.91, bf16[1024,1024]{0,1:T(8,128)(2,1)S(1)} %get-tuple-element.356, bf16[4,1024,128]{2,1,0:T(8,128)(2,1)} %get-tuple-element.422), kind=kOutput, calls=%fused_computation.10.clone.1 | convolution fusion | flops 268435456 | bytes 2884608 | tf_op jit(solution)/shard_map/while/body/eval_jaxpr/ts,td->sd/dot_general | solution.py:52
  107.4 1.6 fusion.97
  111.0 5.2 %bitcast_reduce_fusion.2 = (f32[1024,16]{0,1:T(8,128)S(1)}, f32[1024,1024]{0,1:T(8,128)}, f32[1024,1024]{0,1:T(8,128)}) fusion(f32[1024,1024]{0,1:T(8,128)S(1)} %fusion.91, bf16[4,1024,128]{2,1,0:T(8,128)(2,1)S(1)} %get-tuple-element.423, s32[]{:T(128)S(6)} %copy.91, bf16[4,1024,128]{2,1,0:T(8,128)(2,1)} %get-tuple-element.422), kind=kOutput, calls=%fused_computation.clone.1 | convolution fusion | flops 270516224 | bytes 13173760 | tf_op jit(solution)/shard_map/while/body/eval_jaxpr/td,sd->ts/dot_general | solution.py:46
  118.3 3.2 %select_reduce_fusion.18 = (f32[1024,64]{0,1:T(8,128)S(1)}, f32[1024,16,64]{0,2,1:T(8,128)S(1)}) fusion(f32[1024,16,64]{0,2,1:T(8,128)} %bitcast.218, pred[1024,16]{0,1:T(8,128)(4,1)S(1)} %iota_compare_fusion.4, f32[1024,16]{0,1:T(8,128)S(1)} %get-tuple-element.344, f32[1024,64]{0,1:T(8,128)S(1)} %select_select_fusion.3), kind=kLoop, calls=%fused_computation.5.clone.1 | loop fusion | flops 3080192 | bytes 8994816 | tf_op jit(solution)/shard_map/while/body/eval_jaxpr/reduce_sum | solution.py:56
  123.2 1.8 %fusion.93 = (bf16[1024,1024]{0,1:T(8,128)(2,1)S(1)}, bf16[1024,1024]{0,1:T(8,128)(2,1)S(1)}) fusion(f32[1024,1024]{0,1:T(8,128)S(1)} %copy-done.3, f32[1024,16,64]{0,2,1:T(8,128)S(1)} %get-tuple-element.353, f32[1024,1024]{0,1:T(8,128)S(1)} %copy-done.4), kind=kLoop, calls=%fused_computation.4.clone.1 | loop fusion | flops 4194304 | bytes 16777216 | tf_op jit(solution)/shard_map/while/body/eval_jaxpr/convert_element_type | solution.py:49
  125.0 1.3 fusion.94
  126.3 1.3 fusion.95
  127.6 2.7 %fusion.96 = f32[4,1024,128]{1,2,0:T(8,128)} fusion(f32[4,1024,128]{1,2,0:T(8,128)} %get-tuple-element.395, s32[]{:T(128)S(6)} %copy.91, bf16[1024,1024]{0,1:T(8,128)(2,1)S(1)} %get-tuple-element.356, bf16[4,1024,128]{2,1,0:T(8,128)(2,1)} %get-tuple-element.422), kind=kOutput, calls=%fused_computation.10.clone.1 | convolution fusion | flops 268435456 | bytes 2884608 | tf_op jit(solution)/shard_map/while/body/eval_jaxpr/ts,td->sd/dot_general | solution.py:52
  130.3 1.6 fusion.97
  133.9 1.7 bitcast_multiply_fusion.5
  135.6 3.3 %bitcast_convert_fusion = f32[32,4,128,128]{3,2,1,0:T(8,128)S(1)} fusion(bf16[32,1,4,128,128]{4,3,2,1,0:T(8,128)(2,1)} %all-to-all-done), kind=kLoop, calls=%fused_computation.115 | loop fusion | flops 2097152 | bytes 12582912 | tf_op jit(solution)/shard_map/convert_element_type | solution.py:104
  138.9 5.6 %select_reduce_fusion.13 = bf16[5,4,128,128]{3,2,1,0:T(8,128)(2,1)S(1)} fusion(f32[32,4,128,128]{3,2,1,0:T(8,128)S(1)} %bitcast_convert_fusion, pred[5,32]{1,0:T(8,128)(4,1)S(1)} %broadcast_compare_fusion.12), kind=kLoop, calls=%fused_computation.104 | loop fusion | flops 20643840 | bytes 9044128 | tf_op jit(solution)/shard_map/reduce_sum | solution.py:98
  144.5 1.5 fusion.37
  146.4 3.5 %fusion.39 = (f32[5,4,1024]{2,0,1:T(8,128)}, f32[4,1024,128]{1,2,0:T(8,128)S(1)}) fusion(f32[4,1024,128]{1,2,0:T(8,128)S(1)} %copy-done.13, f32[5,4,1024]{2,0,1:T(8,128)S(1)} %copy-done.20, bf16[4,1024,128]{2,1,0:T(8,128)(2,1)S(1)} %copy-done.10, bf16[5,4,128,128]{3,2,1,0:T(8,128)(2,1)S(1)} %select_reduce_fusion.13), kind=kOutput, calls=%fused_computation.110 | convolution fusion | flops 681029632 | bytes 6062080 | tf_op jit(solution)/shard_map/hcd,bhde->bhce/dot_general | solution.py:125
  150.0 1.7 add_convert_fusion
  151.7 2.3 %copy.49 = bf16[4,1024,128]{2,1,0:T(8,128)(2,1)} copy(bf16[4,1024,128]{1,2,0:T(8,128)(2,1)} %get-tuple-element.237) | data formatting | bytes 2097152
  158.0 2.1 %fusion.44 = bf16[4,1024,128]{1,2,0:T(8,128)(2,1)S(1)} fusion(f32[4,1024,128]{1,2,0:T(8,128)} %get-tuple-element.448, bf16[4,1024,128]{2,1,0:T(8,128)(2,1)S(1)} %get-tuple-element.454, bf16[1,4,128,128]{3,2,1,0:T(8,128)(2,1)} %reduce-scatter.2.cloned.1.call-done), kind=kOutput, calls=%fused_computation.119 | convolution fusion | flops 135266304 | bytes 4325376 | tf_op jit(solution)/shard_map/hde,hce->hcd/dot_general | solution.py:138
  160.1 1.3 copy.51
  161.5 2.1 %fusion.43 = bf16[4,1024,128]{1,2,0:T(8,128)(2,1)S(1)} fusion(f32[4,1024,128]{1,2,0:T(8,128)} %get-tuple-element.449, bf16[4,1024,128]{2,1,0:T(8,128)(2,1)S(1)} %get-tuple-element.453, bf16[1,4,128,128]{3,2,1,0:T(8,128)(2,1)S(1)} %copy-done.14), kind=kOutput, calls=%fused_computation.117 | convolution fusion | flops 135266304 | bytes 4325376 | tf_op jit(solution)/shard_map/hde,hcd->hce/dot_general | solution.py:142
  163.5 1.3 copy.52
  (143 shorter events, 28.8 us)
Async XLA Ops:
  7.2 21.9 %copy-start = (s32[32,32]{1,0:T(8,128)S(1)}, s32[32,32]{1,0:T(8,128)}, u32[]{:S(2)}) copy-start(s32[32,32]{1,0:T(8,128)} %param.13) | copy-start | bytes 12292
  12.2 8.9 %copy-start.18 = (f32[16,4,1024]{2,1,0:T(4,128)S(1)}, f32[16,4,1024]{2,1,0:T(4,128)}, u32[]{:S(2)}) copy-start(f32[16,4,1024]{2,1,0:T(4,128)} %param.12) | copy-start | bytes 786436
  12.2 9.1 %copy-start.7 = (bf16[4,1024,128]{2,1,0:T(8,128)(2,1)S(1)}, bf16[4,1024,128]{2,1,0:T(8,128)(2,1)}, u32[]{:S(2)}) copy-start(bf16[4,1024,128]{2,1,0:T(8,128)(2,1)} %param.11) | copy-start | bytes 3145732
  12.2 123.4 %all-to-all-start = ((bf16[32,1,4,128,128]{4,3,2,1,0:T(8,128)(2,1)}), bf16[32,1,4,128,128]{4,3,2,1,0:T(8,128)(2,1)}, u32[]{:S(2)}, u32[]{:S(2)}) async-start(bf16[32,1,4,128,128]{4,3,2,1,0:T(8,128)(2,1)} %stack.75), calls=%async_computation | async-start | bytes 8388608 | tf_op jit(solution)/shard_map/all_to_all | solution.py:102
  21.0 2.0 %copy-start.9 = (bf16[4,1024,128]{2,1,0:T(8,128)(2,1)S(1)}, bf16[4,1024,128]{2,1,0:T(8,128)(2,1)}, u32[]{:S(2)}) copy-start(bf16[4,1024,128]{2,1,0:T(8,128)(2,1)} %param.8) | copy-start | bytes 3145732
  21.0 137.0 %reduce-scatter.2.cloned.1.call-start = ((), (), s32[]{:S(2)}) async-start(), calls=%async_computation.2 | async-start | bytes 4325376 | tf_op jit(solution)/shard_map/reduce_scatter | solution.py:111
  21.1 8.0 %copy-start.21 = (s32[5]{0:T(128)}, s32[5]{0:T(128)S(1)}, u32[]{:S(2)}) copy-start(s32[5]{0:T(128)S(1)} %iota_add_fusion) | copy-start | bytes 64
  21.3 1.7 %copy-start.19 = (f32[5,4,1024]{2,0,1:T(8,128)}, f32[5,4,1024]{2,0,1:T(8,128)S(1)}, u32[]{:S(2)}) copy-start(f32[5,4,1024]{2,0,1:T(8,128)S(1)} %slice.86) | copy-start | bytes 245764
  29.1 10.5 %copy-start.22 = (s32[32]{0:T(128)}, s32[32]{0:T(128)S(1)}, u32[]{:S(2)}) copy-start(s32[32]{0:T(128)S(1)} %dynamic-slice_bitcast_fusion) | copy-start | bytes 388
  39.6 1.3 copy-start.5
  39.6 1.6 copy-start.6
  41.9 5.2 %copy-start.2 = (f32[1024,1024]{0,1:T(8,128)}, f32[1024,1024]{0,1:T(8,128)S(1)}, u32[]{:S(2)}) copy-start(f32[1024,1024]{0,1:T(8,128)S(1)} %fusion.91) | copy-start | bytes 12582916 | tf_op jit(solution)/shard_map/while
  49.3 3.5 %copy-start.3 = (f32[1024,1024]{0,1:T(8,128)S(1)}, f32[1024,1024]{0,1:T(8,128)}, u32[]{:S(2)}) copy-start(f32[1024,1024]{0,1:T(8,128)} %copy-done.2) | copy-start | bytes 12582916 | tf_op jit(solution)/shard_map/while
  49.3 4.8 %copy-start.4 = (f32[1024,1024]{0,1:T(8,128)S(1)}, f32[1024,1024]{0,1:T(8,128)}, u32[]{:S(2)}) copy-start(f32[1024,1024]{0,1:T(8,128)} %get-tuple-element.354) | copy-start | bytes 12582916 | tf_op jit(solution)/shard_map/while
  58.6 2.7 %copy-start.8 = (bf16[4,1024,128]{2,1,0:T(8,128)(2,1)S(1)}, bf16[4,1024,128]{2,1,0:T(8,128)(2,1)}, u32[]{:S(2)}) copy-start(bf16[4,1024,128]{2,1,0:T(8,128)(2,1)} %get-tuple-element.468) | copy-start | bytes 3145732 | tf_op jit(solution)/shard_map/while
  61.3 2.1 %copy-start.15 = (f32[1024]{0:T(1024)S(1)}, f32[1024]{0:T(1024)}, u32[]{:S(2)}) copy-start(f32[1024]{0:T(1024)} %get-tuple-element.367) | copy-start | bytes 12292 | tf_op jit(solution)/shard_map/while
  61.3 2.1 %copy-start.16 = (f32[1024]{0:T(1024)S(1)}, f32[1024]{0:T(1024)}, u32[]{:S(2)}) copy-start(f32[1024]{0:T(1024)} %get-tuple-element.366) | copy-start | bytes 12292 | tf_op jit(solution)/shard_map/while
  61.3 2.1 %copy-start.17 = (f32[1024]{0:T(1024)S(1)}, f32[1024]{0:T(1024)}, u32[]{:S(2)}) copy-start(f32[1024]{0:T(1024)} %get-tuple-element.365) | copy-start | bytes 12292 | tf_op jit(solution)/shard_map/while
  64.9 5.2 %copy-start.2 = (f32[1024,1024]{0,1:T(8,128)}, f32[1024,1024]{0,1:T(8,128)S(1)}, u32[]{:S(2)}) copy-start(f32[1024,1024]{0,1:T(8,128)S(1)} %fusion.91) | copy-start | bytes 12582916 | tf_op jit(solution)/shard_map/while
  72.2 3.7 %copy-start.3 = (f32[1024,1024]{0,1:T(8,128)S(1)}, f32[1024,1024]{0,1:T(8,128)}, u32[]{:S(2)}) copy-start(f32[1024,1024]{0,1:T(8,128)} %copy-done.2) | copy-start | bytes 12582916 | tf_op jit(solution)/shard_map/while
  72.2 5.1 %copy-start.4 = (f32[1024,1024]{0,1:T(8,128)S(1)}, f32[1024,1024]{0,1:T(8,128)}, u32[]{:S(2)}) copy-start(f32[1024,1024]{0,1:T(8,128)} %get-tuple-element.354) | copy-start | bytes 12582916 | tf_op jit(solution)/shard_map/while
  81.9 2.7 %copy-start.8 = (bf16[4,1024,128]{2,1,0:T(8,128)(2,1)S(1)}, bf16[4,1024,128]{2,1,0:T(8,128)(2,1)}, u32[]{:S(2)}) copy-start(bf16[4,1024,128]{2,1,0:T(8,128)(2,1)} %get-tuple-element.468) | copy-start | bytes 3145732 | tf_op jit(solution)/shard_map/while
  84.5 2.1 %copy-start.15 = (f32[1024]{0:T(1024)S(1)}, f32[1024]{0:T(1024)}, u32[]{:S(2)}) copy-start(f32[1024]{0:T(1024)} %get-tuple-element.367) | copy-start | bytes 12292 | tf_op jit(solution)/shard_map/while
  84.5 2.1 %copy-start.16 = (f32[1024]{0:T(1024)S(1)}, f32[1024]{0:T(1024)}, u32[]{:S(2)}) copy-start(f32[1024]{0:T(1024)} %get-tuple-element.366) | copy-start | bytes 12292 | tf_op jit(solution)/shard_map/while
  84.5 2.1 %copy-start.17 = (f32[1024]{0:T(1024)S(1)}, f32[1024]{0:T(1024)}, u32[]{:S(2)}) copy-start(f32[1024]{0:T(1024)} %get-tuple-element.365) | copy-start | bytes 12292 | tf_op jit(solution)/shard_map/while
  88.1 5.2 %copy-start.2 = (f32[1024,1024]{0,1:T(8,128)}, f32[1024,1024]{0,1:T(8,128)S(1)}, u32[]{:S(2)}) copy-start(f32[1024,1024]{0,1:T(8,128)S(1)} %fusion.91) | copy-start | bytes 12582916 | tf_op jit(solution)/shard_map/while
  95.5 3.5 %copy-start.3 = (f32[1024,1024]{0,1:T(8,128)S(1)}, f32[1024,1024]{0,1:T(8,128)}, u32[]{:S(2)}) copy-start(f32[1024,1024]{0,1:T(8,128)} %copy-done.2) | copy-start | bytes 12582916 | tf_op jit(solution)/shard_map/while
  95.5 4.8 %copy-start.4 = (f32[1024,1024]{0,1:T(8,128)S(1)}, f32[1024,1024]{0,1:T(8,128)}, u32[]{:S(2)}) copy-start(f32[1024,1024]{0,1:T(8,128)} %get-tuple-element.354) | copy-start | bytes 12582916 | tf_op jit(solution)/shard_map/while
  104.7 2.7 %copy-start.8 = (bf16[4,1024,128]{2,1,0:T(8,128)(2,1)S(1)}, bf16[4,1024,128]{2,1,0:T(8,128)(2,1)}, u32[]{:S(2)}) copy-start(bf16[4,1024,128]{2,1,0:T(8,128)(2,1)} %get-tuple-element.468) | copy-start | bytes 3145732 | tf_op jit(solution)/shard_map/while
  107.4 2.1 %copy-start.15 = (f32[1024]{0:T(1024)S(1)}, f32[1024]{0:T(1024)}, u32[]{:S(2)}) copy-start(f32[1024]{0:T(1024)} %get-tuple-element.367) | copy-start | bytes 12292 | tf_op jit(solution)/shard_map/while
  107.4 2.1 %copy-start.16 = (f32[1024]{0:T(1024)S(1)}, f32[1024]{0:T(1024)}, u32[]{:S(2)}) copy-start(f32[1024]{0:T(1024)} %get-tuple-element.366) | copy-start | bytes 12292 | tf_op jit(solution)/shard_map/while
  107.4 2.1 %copy-start.17 = (f32[1024]{0:T(1024)S(1)}, f32[1024]{0:T(1024)}, u32[]{:S(2)}) copy-start(f32[1024]{0:T(1024)} %get-tuple-element.365) | copy-start | bytes 12292 | tf_op jit(solution)/shard_map/while
  111.0 5.2 %copy-start.2 = (f32[1024,1024]{0,1:T(8,128)}, f32[1024,1024]{0,1:T(8,128)S(1)}, u32[]{:S(2)}) copy-start(f32[1024,1024]{0,1:T(8,128)S(1)} %fusion.91) | copy-start | bytes 12582916 | tf_op jit(solution)/shard_map/while
  118.3 3.6 %copy-start.3 = (f32[1024,1024]{0,1:T(8,128)S(1)}, f32[1024,1024]{0,1:T(8,128)}, u32[]{:S(2)}) copy-start(f32[1024,1024]{0,1:T(8,128)} %copy-done.2) | copy-start | bytes 12582916 | tf_op jit(solution)/shard_map/while
  118.3 4.8 %copy-start.4 = (f32[1024,1024]{0,1:T(8,128)S(1)}, f32[1024,1024]{0,1:T(8,128)}, u32[]{:S(2)}) copy-start(f32[1024,1024]{0,1:T(8,128)} %get-tuple-element.354) | copy-start | bytes 12582916 | tf_op jit(solution)/shard_map/while
  127.6 2.7 %copy-start.8 = (bf16[4,1024,128]{2,1,0:T(8,128)(2,1)S(1)}, bf16[4,1024,128]{2,1,0:T(8,128)(2,1)}, u32[]{:S(2)}) copy-start(bf16[4,1024,128]{2,1,0:T(8,128)(2,1)} %get-tuple-element.468) | copy-start | bytes 3145732 | tf_op jit(solution)/shard_map/while
  130.3 2.1 %copy-start.15 = (f32[1024]{0:T(1024)S(1)}, f32[1024]{0:T(1024)}, u32[]{:S(2)}) copy-start(f32[1024]{0:T(1024)} %get-tuple-element.367) | copy-start | bytes 12292 | tf_op jit(solution)/shard_map/while
  130.3 2.1 %copy-start.16 = (f32[1024]{0:T(1024)S(1)}, f32[1024]{0:T(1024)}, u32[]{:S(2)}) copy-start(f32[1024]{0:T(1024)} %get-tuple-element.366) | copy-start | bytes 12292 | tf_op jit(solution)/shard_map/while
  130.3 2.1 %copy-start.17 = (f32[1024]{0:T(1024)S(1)}, f32[1024]{0:T(1024)}, u32[]{:S(2)}) copy-start(f32[1024]{0:T(1024)} %get-tuple-element.365) | copy-start | bytes 12292 | tf_op jit(solution)/shard_map/while
  138.9 5.6 %copy-start.20 = (f32[5,4,1024]{2,0,1:T(8,128)S(1)}, f32[5,4,1024]{2,0,1:T(8,128)}, u32[]{:S(2)}) copy-start(f32[5,4,1024]{2,0,1:T(8,128)} %copy-done.19) | copy-start | bytes 245764
  144.5 1.6 copy-start.10
  144.5 1.9 %copy-start.13 = (f32[4,1024,128]{1,2,0:T(8,128)S(1)}, f32[4,1024,128]{1,2,0:T(8,128)}, u32[]{:S(2)}) copy-start(f32[4,1024,128]{1,2,0:T(8,128)} %copy.44) | copy-start | bytes 6291460
  146.4 3.5 %copy-start.11 = (f32[4,1024,128]{1,2,0:T(8,128)S(1)}, f32[4,1024,128]{1,2,0:T(8,128)}, u32[]{:S(2)}) copy-start(f32[4,1024,128]{1,2,0:T(8,128)} %get-tuple-element.446) | copy-start | bytes 6291460
  146.4 3.5 %copy-start.12 = (f32[4,1024,128]{1,2,0:T(8,128)S(1)}, f32[4,1024,128]{1,2,0:T(8,128)}, u32[]{:S(2)}) copy-start(f32[4,1024,128]{1,2,0:T(8,128)} %get-tuple-element.447) | copy-start | bytes 6291460
  160.1 1.3 copy-start.14
  161.4 3.4 %copy-start.1 = (s32[32,32]{1,0:T(8,128)S(1)}, s32[32,32]{1,0:T(8,128)}, u32[]{:S(2)}) copy-start(s32[32,32]{1,0:T(8,128)} %param.13) | copy-start | bytes 12292
Sparse Core Ops, SparseCore 0:
  39.7 90.5 reduce-scatter.1
